TPU v7x, 512 devices: a whole 4x4x16 slice. The times are simulated.
512 devices in a mesh: context: 128 (over z, y, core), tensor: 4 (over x).
Axes of the slice: x: 4, y: 4, z: 16, core: 2. Of those that a mesh axis runs over, the one named last changes fastest.
Arguments:
- projected: bfloat16 [3, 16, 512, 16384], P(None, 'tensor', None, 'context'), may hold values from -6 to 6
- long_filter: bfloat16 [512, 128], replicated, may hold values from -0.5 to 0.5
- cotangent: bfloat16 [16, 512, 16384], P('tensor', None, 'context'), may hold values from -6 to 6
Outputs:
- mixed: bfloat16 [16, 512, 16384], P('tensor', None, 'context')
- stream_grads: bfloat16 [3, 16, 512, 16384], P(None, 'tensor', None, 'context')
- filter_grads: float32 [512, 128], P('context')
All inputs are finite; a program needn't handle non-finite values.
Results may differ from a plain program's by a relative error of at most 0.0057.
Values may be sent and summed in bfloat16 or wider, within the bound.
No kernel may reach another device: no remote copies, remote signals or barrier semaphores. Data moves between devices by JAX's collectives and lax.ppermute only.
A program may use at most 64 MiB of HBM per device.

v0:
```python
import math
import jax
import jax.numpy as jnp
from jax import lax
from jax.sharding import PartitionSpec as P


def selector_table(filter_taps):
    rows = lax.broadcasted_iota(jnp.int32, (filter_taps, filter_taps), 0)
    cols = lax.broadcasted_iota(jnp.int32, (filter_taps, filter_taps), 1)
    offset = (rows - cols + filter_taps) % filter_taps
    taps = lax.broadcasted_iota(jnp.int32, (filter_taps, filter_taps, filter_taps), 0)
    table = (offset[None, :, :] == taps).astype(jnp.bfloat16)
    return (table.reshape(filter_taps, filter_taps * filter_taps), rows >= cols)


def conv_both(tiles, earlier, grad_tiles, grad_next, filters):
    groups, filter_taps = filters.shape
    block_width = math.gcd(groups, 32)
    table, lower = selector_table(filter_taps)
    table_wide = table.astype(jnp.float32)

    def advance(index, carry):
        circulant = jnp.dot(filters, table, preferred_element_type=jnp.float32).reshape(
            block_width, filter_taps, filter_taps
        )
        low_band = jnp.where(lower[None], circulant, 0.0).astype(jnp.bfloat16)
        high_band = jnp.where(lower[None], 0.0, circulant).astype(jnp.bfloat16)
        forward = jnp.einsum("mgbk,gik->mgbi", tiles, low_band, preferred_element_type=jnp.float32)
        forward = forward + jnp.einsum(
            "mgbk,gik->mgbi", earlier, high_band, preferred_element_type=jnp.float32
        )
        backward = jnp.einsum(
            "mgbi,gik->mgbk", grad_tiles, low_band, preferred_element_type=jnp.float32
        )
        backward = backward + jnp.einsum(
            "mgbi,gik->mgbk", grad_next, high_band, preferred_element_type=jnp.float32
        )
        outer_low = jnp.einsum(
            "mgbi,mgbk->gik", grad_tiles, tiles, preferred_element_type=jnp.float32
        )
        outer_high = jnp.einsum(
            "mgbi,mgbk->gik", grad_tiles, earlier, preferred_element_type=jnp.float32
        )
        merged = jnp.where(lower[None], outer_low, outer_high).reshape(
            block_width, filter_taps * filter_taps
        )
        sums = jnp.dot(merged, table_wide.T, precision=lax.Precision.HIGHEST)
        filtered_out = forward.astype(jnp.bfloat16)
        grads_out = backward.astype(jnp.bfloat16)
        return (filtered_out, grads_out, sums)

    initial = (
        jnp.zeros(tiles.shape, jnp.bfloat16),
        jnp.zeros(tiles.shape, jnp.bfloat16),
        jnp.zeros((groups, filter_taps), jnp.float32),
    )
    return lax.fori_loop(0, groups // block_width, advance, initial)


def shifted_tiles(tiles, before, grad_tiles, after):
    earlier = jnp.concatenate([before, tiles[:, :, :-1]], 2)
    grad_next = jnp.concatenate([grad_tiles[:, :, 1:], after], 2)
    return (earlier, grad_next)


def channel_filters(long_filter, own_groups):
    first_group = lax.axis_index("context") * own_groups
    return lax.dynamic_slice_in_dim(long_filter, first_group, own_groups, 0)


def channel_conv(columns, grad_columns, long_filter, filter_taps):
    members, own_groups, length = columns.shape
    filters = channel_filters(long_filter, own_groups)
    tiles = columns.reshape(members, own_groups, length // filter_taps, filter_taps)
    grad_tiles = grad_columns.reshape(members, own_groups, length // filter_taps, filter_taps)
    blank = jnp.zeros((members, own_groups, 1, filter_taps), jnp.bfloat16)
    earlier, grad_next = shifted_tiles(tiles, blank, grad_tiles, blank)
    filtered_tiles, gated_tiles, partial_taps = conv_both(
        tiles, earlier, grad_tiles, grad_next, filters
    )
    return (
        filtered_tiles.reshape(members, own_groups, length),
        gated_tiles.reshape(members, own_groups, length),
        partial_taps,
    )


def body(projected, long_filter, cotangent):
    filter_taps = long_filter.shape[1]
    query_stream = projected[0]
    key_stream = projected[1]
    value_stream = projected[2]
    gated = (key_stream.astype(jnp.float32) * value_stream.astype(jnp.float32)).astype(jnp.bfloat16)
    members, groups, local_tokens = gated.shape
    length = local_tokens * lax.axis_size("context")
    factor = 1.0 / math.sqrt(members * lax.axis_size("tensor") * length)
    grad_filtered = (cotangent.astype(jnp.float32) * query_stream.astype(jnp.float32)).astype(
        jnp.bfloat16
    )
    columns = lax.all_to_all(gated, "context", split_axis=1, concat_axis=2, tiled=True)
    grad_columns = lax.all_to_all(grad_filtered, "context", split_axis=1, concat_axis=2, tiled=True)
    filtered_columns, gated_columns, partial_taps = channel_conv(
        columns, grad_columns, long_filter, filter_taps
    )
    filtered = lax.all_to_all(filtered_columns, "context", split_axis=2, concat_axis=1, tiled=True)
    grad_gated = lax.all_to_all(gated_columns, "context", split_axis=2, concat_axis=1, tiled=True)
    filter_grads = lax.psum(partial_taps, "tensor") * factor
    filtered_wide = filtered.astype(jnp.float32)
    grad_wide = grad_gated.astype(jnp.float32)
    mixed = (query_stream.astype(jnp.float32) * filtered_wide).astype(jnp.bfloat16)
    stream_grads = jnp.stack(
        [
            cotangent.astype(jnp.float32) * filtered_wide,
            grad_wide * value_stream.astype(jnp.float32),
            grad_wide * key_stream.astype(jnp.float32),
        ]
    ).astype(jnp.bfloat16)
    return (mixed, stream_grads, filter_grads)


def solution(mesh):
    in_specs = (P(None, "tensor", None, "context"), P(), P("tensor", None, "context"))
    out_specs = (
        P("tensor", None, "context"),
        P(None, "tensor", None, "context"),
        P("context", None),
    )
    return jax.shard_map(body, mesh=mesh, in_specs=in_specs, out_specs=out_specs, check_vma=False)
```

profile of v0, /device:TPU:39, one launch (start us, length us, event | category | flops | bytes accessed | tf_op | source)
XLA Modules:
  0.0 418.9 jit_solution(2552468281968310351)
XLA Ops:
  0.6 2.3 fusion.32
  2.9 1.5 fusion.15
  4.4 19.5 %all-to-all-start = ((bf16[4,512,128]{2,0,1:T(4,128)(2,1)}), bf16[4,512,128]{2,0,1:T(4,128)(2,1)S(1)}, u32[]{:S(2)}, u32[]{:S(2)}) async-start(bf16[4,512,128]{2,0,1:T(4,128)(2,1)} %fusion.15), calls=%async_computation | async-start | bytes 1048576 | tf_op jit(solution)/shard_map/all_to_all | solution.py:101
  24.0 3.7 fusion.21
  28.0 29.5 %all-to-all-done = bf16[4,512,128]{2,0,1:T(4,128)(2,1)S(1)} async-done(((bf16[4,512,128]{2,0,1:T(4,128)(2,1)}), bf16[4,512,128]{2,0,1:T(4,128)(2,1)S(1)}, u32[]{:S(2)}, u32[]{:S(2)}) %all-to-all-start) | async-done | bytes 524320 | tf_op jit(solution)/shard_map/all_to_all | solution.py:101
  58.3 26.7 %copy.58 = bf16[4,4,128,128]{1,0,3,2:T(4,128)(2,1)} copy(bf16[4,4,128,128]{2,3,0,1:T(8,128)(2,1)S(1)} %fusion.7) | data formatting | bytes 1048576 | tf_op jit(solution)/shard_map/reshape | solution.py:83
  85.1 31.2 %reshape.98 = bf16[128,2,1024]{2,1,0:T(2,128)(2,1)S(1)} reshape(bf16[16384,4,4]{2,1,0:T(4,128)(2,1)} %bitcast.75) | data formatting | bytes 1048576
  116.2 39.7 %all_to_all.48 = bf16[128,2,1024]{2,1,0:T(2,128)(2,1)S(1)} all-to-all(bf16[128,2,1024]{2,1,0:T(2,128)(2,1)S(1)} %reshape.98), channel_id=1, replica_groups=mesh['context'=128,'tensor'=4] {'context'}, dimensions={0} | all-to-all | bytes 1048576 | tf_op jit(solution)/shard_map/all_to_all | solution.py:106
  156.0 37.0 %reshape.99 = bf16[16384,4,4]{2,1,0:T(4,128)(2,1)} reshape(bf16[128,2,1024]{2,1,0:T(2,128)(2,1)S(1)} %all_to_all.48) | data formatting | bytes 1048576
  193.0 21.7 %copy.29 = f32[4,4,128,128]{3,0,1,2:T(4,128)} copy(bf16[4,4,128,128]{1,0,3,2:T(4,128)(2,1)} %bitcast.76) | data formatting | bytes 1572864 | tf_op jit(solution)/shard_map/convert_element_type | solution.py:109
  214.7 3.2 fusion.12
  217.9 39.9 %all_to_all.49 = bf16[4,512,128]{2,0,1:T(4,128)(2,1)S(1)} all-to-all(bf16[4,512,128]{2,0,1:T(4,128)(2,1)S(1)} %get-tuple-element.32), channel_id=1, replica_groups=mesh['context'=128,'tensor'=4] {'context'}, dimensions={1} | all-to-all | bytes 1048576 | tf_op jit(solution)/shard_map/all_to_all | solution.py:102
  258.7 26.7 %copy.65 = bf16[4,4,128,128]{1,0,3,2:T(4,128)(2,1)} copy(bf16[4,4,128,128]{2,3,0,1:T(8,128)(2,1)S(1)} %fusion.6) | data formatting | bytes 1048576 | tf_op jit(solution)/shard_map/reshape | solution.py:84
  285.4 31.8 %reshape.100 = bf16[128,2,1024]{2,1,0:T(2,128)(2,1)} reshape(bf16[16384,4,4]{2,1,0:T(4,128)(2,1)} %bitcast.77) | data formatting | bytes 1048576
  317.2 6.3 %all-to-all-start.3 = ((bf16[128,2,1024]{2,1,0:T(2,128)(2,1)}), bf16[128,2,1024]{2,1,0:T(2,128)(2,1)S(1)}, u32[]{:S(2)}, u32[]{:S(2)}) async-start(bf16[128,2,1024]{2,1,0:T(2,128)(2,1)} %reshape.100), calls=%async_computation.3 | async-start | bytes 1048576 | tf_op jit(solution)/shard_map/all_to_all | solution.py:107
  323.6 1.9 copy.42
  326.2 4.1 fusion.8
  330.4 6.3 %psum.7 = f32[4,128]{1,0:T(4,128)S(1)} all-reduce(f32[4,128]{1,0:T(4,128)S(1)} %fusion.8), channel_id=1, replica_groups=mesh['context'=128,'tensor'=4] {'tensor'}, use_global_device_ids=true, to_apply=%region_0.1 | all-reduce | flops 512 | bytes 4096 | tf_op jit(solution)/shard_map/psum | solution.py:108
  337.2 20.0 %all-to-all-done.3 = bf16[128,2,1024]{2,1,0:T(2,128)(2,1)S(1)} async-done(((bf16[128,2,1024]{2,1,0:T(2,128)(2,1)}), bf16[128,2,1024]{2,1,0:T(2,128)(2,1)S(1)}, u32[]{:S(2)}, u32[]{:S(2)}) %all-to-all-start.3) | async-done | bytes 524320 | tf_op jit(solution)/shard_map/all_to_all | solution.py:107
  357.2 37.0 %reshape.101 = bf16[16384,4,4]{2,1,0:T(4,128)(2,1)} reshape(bf16[128,2,1024]{2,1,0:T(2,128)(2,1)S(1)} %all-to-all-done.3) | data formatting | bytes 1048576
  394.2 21.0 %copy.37 = f32[4,4,128,128]{3,0,1,2:T(4,128)S(1)} copy(bf16[4,4,128,128]{1,0,3,2:T(4,128)(2,1)} %bitcast.78) | data formatting | bytes 1572864 | tf_op jit(solution)/shard_map/convert_element_type | solution.py:110
  415.2 1.0 fusion.11
  416.2 1.3 pad_maximum_fusion
  417.5 1.4 copy.43
  (24 shorter events, 3.5 us)
Async XLA Ops:
  0.6 23.3 %copy-start = (bf16[512,128]{1,0:T(8,128)(2,1)S(1)}, bf16[512,128]{1,0:T(8,128)(2,1)}, u32[]{:S(2)}) copy-start(bf16[512,128]{1,0:T(8,128)(2,1)} %param.4) | copy-start | bytes 393220
  4.4 53.1 %all-to-all-start = ((bf16[4,512,128]{2,0,1:T(4,128)(2,1)}), bf16[4,512,128]{2,0,1:T(4,128)(2,1)S(1)}, u32[]{:S(2)}, u32[]{:S(2)}) async-start(bf16[4,512,128]{2,0,1:T(4,128)(2,1)} %fusion.15), calls=%async_computation | async-start | bytes 1048576 | tf_op jit(solution)/shard_map/all_to_all | solution.py:101
  193.0 21.7 %copy-start.2 = (bf16[1,4,512,128]{3,2,1,0:T(8,128)(2,1)S(1)}, bf16[1,4,512,128]{3,2,1,0:T(8,128)(2,1)}, u32[]{:S(2)}) copy-start(bf16[1,4,512,128]{3,2,1,0:T(8,128)(2,1)} %get-tuple-element.27) | copy-start | bytes 1572868
  193.0 21.7 %copy-start.4 = (bf16[4,512,128]{2,1,0:T(8,128)(2,1)S(1)}, bf16[4,512,128]{2,1,0:T(8,128)(2,1)}, u32[]{:S(2)}) copy-start(bf16[4,512,128]{2,1,0:T(8,128)(2,1)} %param.5) | copy-start | bytes 1572868
  317.2 39.9 %all-to-all-start.3 = ((bf16[128,2,1024]{2,1,0:T(2,128)(2,1)}), bf16[128,2,1024]{2,1,0:T(2,128)(2,1)S(1)}, u32[]{:S(2)}, u32[]{:S(2)}) async-start(bf16[128,2,1024]{2,1,0:T(2,128)(2,1)} %reshape.100), calls=%async_computation.3 | async-start | bytes 1048576 | tf_op jit(solution)/shard_map/all_to_all | solution.py:107
  415.2 1.0 copy-start.3
  416.2 2.7 copy-start.1
where the time goes:
time: 420 us; the launch traced here: 419 us
  local copies, waits for them, and re-layouts  239 us (57%)
  blocking collectives  85.9 us (20%)
  waiting for transfers between devices  49.5 us (12%)
  starting transfers between devices  25.8 us (6%)
  matrix products  9.88 us (2%)
  other arithmetic  7.57 us (2%)
    unnamed x16, local copies, waits for them, and re-layouts  140 us
    all_to_all x1, blocking collectives, body(): lax.all_to_all(grad_filtered, 'context', split_axis=1, concat_axis=2, til...  39.9 us
    all_to_all x1, blocking collectives, body(): lax.all_to_all(filtered_columns, 'context', split_axis=2, concat_axis=1,...  39.7 us
    all_to_all x1, waiting for transfers between devices, body(): lax.all_to_all(gated, 'context', split_axis=1, concat_axis=2, tiled=True)  29.5 us
    reshape x1, local copies, waits for them, and re-layouts, channel_conv(): filtered_tiles.reshape(members, own_groups, length)  26.7 us
    reshape x1, local copies, waits for them, and re-layouts, channel_conv(): gated_tiles.reshape(members, own_groups, length)  26.7 us
    convert_element_type x1, local copies, waits for them, and re-layouts, body(): filtered_wide = filtered.astype(jnp.float32)  21.7 us
    convert_element_type x1, local copies, waits for them, and re-layouts, body(): grad_wide = grad_gated.astype(jnp.float32)  21 us
  transfers between devices with their start and end apart: 2, of which 2 were waited for; matrix products, arithmetic and copies ran while one was open for 3% of the time, Pallas kernels for 0%

commit v1 on v0

--- a/solution.py
+++ b/solution.py
@@ -104,7 +104,12 @@
         columns, grad_columns, long_filter, filter_taps
     )
     filtered = lax.all_to_all(filtered_columns, "context", split_axis=2, concat_axis=1, tiled=True)
-    grad_gated = lax.all_to_all(gated_columns, "context", split_axis=2, concat_axis=1, tiled=True)
+    grad_gated = jnp.concatenate(
+        lax.all_to_all(
+            jnp.stack(jnp.split(gated_columns, lax.axis_size("context"), axis=2)), "context", 0, 0
+        ),
+        axis=1,
+    )
     filter_grads = lax.psum(partial_taps, "tensor") * factor
     filtered_wide = filtered.astype(jnp.float32)
     grad_wide = grad_gated.astype(jnp.float32)

time: 420 us -> 306 us (0.73)
  the two profiles are of different devices: /device:TPU:39 before, /device:TPU:35 now
where the time goes in v1:
time: 306 us; the launch traced here: 305 us
  local copies, waits for them, and re-layouts  124 us (41%)
  blocking collectives  86.8 us (28%)
  waiting for transfers between devices  49.9 us (16%)
  starting transfers between devices  26.4 us (9%)
  matrix products  10.7 us (3%)
  other arithmetic  5.77 us (2%)
    unnamed x143, local copies, waits for them, and re-layouts  72.7 us
    all_to_all x1, blocking collectives, body(): lax.all_to_all(jnp.stack(jnp.split(gated_columns, lax.axis_size('context'...  39.7 us
    all_to_all x1, blocking collectives, body(): lax.all_to_all(gated, 'context', split_axis=1, concat_axis=2, tiled=True)  39.7 us
    all_to_all x1, waiting for transfers between devices, body(): lax.all_to_all(grad_filtered, 'context', split_axis=1, concat_axis=2, til...  29.5 us
    reshape x1, local copies, waits for them, and re-layouts, channel_conv(): filtered_tiles.reshape(members, own_groups, length)  27.3 us
    convert_element_type x1, local copies, waits for them, and re-layouts, body(): filtered_wide = filtered.astype(jnp.float32)  21.1 us
    all_to_all x1, waiting for transfers between devices, body(): lax.all_to_all(filtered_columns, 'context', split_axis=2, concat_axis=1,...  20.4 us
    all_to_all x1, starting transfers between devices, body(): lax.all_to_all(grad_filtered, 'context', split_axis=1, concat_axis=2, til...  19.5 us
  transfers between devices with their start and end apart: 2, of which 2 were waited for; matrix products, arithmetic and copies ran while one was open for 3% of the time, Pallas kernels for 0%

profile of v1, /device:TPU:35, one launch (start us, length us, event | category | flops | bytes accessed | tf_op | source)
XLA Modules:
  0.0 304.9 jit_solution(11914550479397500090)
XLA Ops:
  0.6 1.4 fusion.14
  2.0 1.2 copy.177
  3.2 19.5 %all-to-all-start.2 = ((bf16[4,512,128]{2,0,1:T(4,128)(2,1)}), bf16[4,512,128]{2,0,1:T(4,128)(2,1)S(1)}, u32[]{:S(2)}, u32[]{:S(2)}) async-start(bf16[4,512,128]{2,0,1:T(4,128)(2,1)} %copy.177), calls=%async_computation.2 | async-start | bytes 1048576 | tf_op jit(solution)/shard_map/all_to_all | solution.py:102
  22.8 3.7 %fusion.22 = (bf16[4,128,128,1]{2,0,1,3:T(4,128)(2,1)S(1)}, bf16[4,128,128,1]{2,0,1,3:T(4,128)(2,1)S(1)}) fusion(pred[128,128]{1,0:T(8,128)(4,1)S(1)} %iota_compare_fusion.6, s32[128,128]{1,0:T(8,128)S(1)} %add_select_fusion, bf16[512,128]{1,0:T(8,128)(2,1)S(1)} %copy-done, s32[]{:T(128)S(6)} %select_n.33), kind=kOutput, calls=%fused_computation.169 | convolution fusion | flops 19005440 | bytes 345092 | tf_op jit(solution)/shard_map/while/body/eval_jaxpr/dot_general | solution.py:24
  26.8 29.5 %all-to-all-done.2 = bf16[4,512,128]{2,0,1:T(4,128)(2,1)S(1)} async-done(((bf16[4,512,128]{2,0,1:T(4,128)(2,1)}), bf16[4,512,128]{2,0,1:T(4,128)(2,1)S(1)}, u32[]{:S(2)}, u32[]{:S(2)}) %all-to-all-start.2) | async-done | bytes 524320 | tf_op jit(solution)/shard_map/all_to_all | solution.py:102
  59.7 39.7 %all_to_all.44 = bf16[128,4,4,128]{3,2,1,0:T(4,128)(2,1)S(1)} all-to-all(bf16[128,4,4,128]{3,2,1,0:T(4,128)(2,1)S(1)} %constant_dynamic-update-slice_fusion), channel_id=1, replica_groups=mesh['context'=128,'tensor'=4] {'context'}, dimensions={0} | all-to-all | bytes 1048576 | tf_op jit(solution)/shard_map/all_to_all | solution.py:108
  99.8 1.1 copy-done.1
  100.8 1.3 fusion.11
  102.2 0.4 copy.169
  102.6 39.7 %all_to_all.45 = bf16[4,512,128]{2,0,1:T(4,128)(2,1)S(1)} all-to-all(bf16[4,512,128]{2,0,1:T(4,128)(2,1)S(1)} %copy.169), channel_id=1, replica_groups=mesh['context'=128,'tensor'=4] {'context'}, dimensions={1} | all-to-all | bytes 1048576 | tf_op jit(solution)/shard_map/all_to_all | solution.py:101
  142.4 0.3 fusion.31
  142.8 1.1 fusion.7
  143.9 27.3 %copy.202 = bf16[4,4,128,128]{1,0,3,2:T(4,128)(2,1)} copy(bf16[4,4,128,128]{2,3,0,1:T(8,128)(2,1)} %fusion.7) | data formatting | bytes 1048576 | tf_op jit(solution)/shard_map/reshape | solution.py:83
  171.3 31.8 %reshape.97 = bf16[128,2,1024]{2,1,0:T(2,128)(2,1)} reshape(bf16[16384,4,4]{2,1,0:T(4,128)(2,1)} %bitcast.578) | data formatting | bytes 1048576
  203.1 6.9 %all-to-all-start.1 = ((bf16[128,2,1024]{2,1,0:T(2,128)(2,1)}), bf16[128,2,1024]{2,1,0:T(2,128)(2,1)}, u32[]{:S(2)}, u32[]{:S(2)}) async-start(bf16[128,2,1024]{2,1,0:T(2,128)(2,1)} %reshape.97), calls=%async_computation.1 | async-start | bytes 1048576 | tf_op jit(solution)/shard_map/all_to_all | solution.py:106
  210.1 0.4 convolution_bitcast_fusion
  210.8 4.1 %fusion.8 = f32[4,128]{1,0:T(4,128)S(1)} fusion(s32[128,128]{1,0:T(8,128)S(1)} %copy-done.6, f32[4,128,128]{2,1,0:T(8,128)S(1)} %convolution_bitcast_fusion, f32[4,128,128]{2,1,0:T(8,128)S(1)} %convolution_bitcast_fusion.1, pred[128,128]{1,0:T(8,128)(4,1)S(1)} %iota_compare_fusion.6), kind=kOutput, calls=%fused_computation.21 | convolution fusion | flops 102825984 | bytes 608256 | tf_op jit(solution)/shard_map/while/body/eval_jaxpr/dot_general | solution.py:48
  215.0 7.4 %psum.7 = f32[4,128]{1,0:T(4,128)S(1)} all-reduce(f32[4,128]{1,0:T(4,128)S(1)} %fusion.8), channel_id=1, replica_groups=mesh['context'=128,'tensor'=4] {'tensor'}, use_global_device_ids=true, to_apply=%region_0.1 | all-reduce | flops 512 | bytes 4096 | tf_op jit(solution)/shard_map/psum | solution.py:113
  222.3 0.6 broadcast_multiply_fusion
  222.9 20.4 %all-to-all-done.1 = bf16[128,2,1024]{2,1,0:T(2,128)(2,1)} async-done(((bf16[128,2,1024]{2,1,0:T(2,128)(2,1)}), bf16[128,2,1024]{2,1,0:T(2,128)(2,1)}, u32[]{:S(2)}, u32[]{:S(2)}) %all-to-all-start.1) | async-done | bytes 524320 | tf_op jit(solution)/shard_map/all_to_all | solution.py:106
  243.3 37.8 %reshape.98 = bf16[16384,4,4]{2,1,0:T(4,128)(2,1)} reshape(bf16[128,2,1024]{2,1,0:T(2,128)(2,1)} %all-to-all-done.1) | data formatting | bytes 1048576
  281.1 21.1 %copy.176 = f32[4,4,128,128]{3,1,2,0:T(4,128)S(1)} copy(bf16[4,4,128,128]{1,0,3,2:T(4,128)(2,1)} %bitcast.579) | data formatting | bytes 1572864 | tf_op jit(solution)/shard_map/convert_element_type | solution.py:114
  302.2 1.0 fusion.15
  303.5 1.3 pad_maximum_fusion
  (155 shorter events, 4.4 us)
Async XLA Ops:
  0.6 22.1 %copy-start = (bf16[512,128]{1,0:T(8,128)(2,1)S(1)}, bf16[512,128]{1,0:T(8,128)(2,1)}, u32[]{:S(2)}) copy-start(bf16[512,128]{1,0:T(8,128)(2,1)} %param.4) | copy-start | bytes 393220
  3.2 53.1 %all-to-all-start.2 = ((bf16[4,512,128]{2,0,1:T(4,128)(2,1)}), bf16[4,512,128]{2,0,1:T(4,128)(2,1)S(1)}, u32[]{:S(2)}, u32[]{:S(2)}) async-start(bf16[4,512,128]{2,0,1:T(4,128)(2,1)} %copy.177), calls=%async_computation.2 | async-start | bytes 1048576 | tf_op jit(solution)/shard_map/all_to_all | solution.py:102
  22.8 33.7 %copy-start.5 = (s32[128,128]{1,0:T(8,128)}, s32[128,128]{1,0:T(8,128)S(1)}, u32[]{:S(2)}) copy-start(s32[128,128]{1,0:T(8,128)S(1)} %add_select_fusion) | copy-start | bytes 196612
  99.4 1.4 copy-start.1
  203.1 7.7 %copy-start.6 = (s32[128,128]{1,0:T(8,128)S(1)}, s32[128,128]{1,0:T(8,128)}, u32[]{:S(2)}) copy-start(s32[128,128]{1,0:T(8,128)} %copy-done.5) | copy-start | bytes 196612
  203.1 40.2 %all-to-all-start.1 = ((bf16[128,2,1024]{2,1,0:T(2,128)(2,1)}), bf16[128,2,1024]{2,1,0:T(2,128)(2,1)}, u32[]{:S(2)}, u32[]{:S(2)}) async-start(bf16[128,2,1024]{2,1,0:T(2,128)(2,1)} %reshape.97), calls=%async_computation.1 | async-start | bytes 1048576 | tf_op jit(solution)/shard_map/all_to_all | solution.py:106
  281.1 21.1 %copy-start.2 = (bf16[4,512,128]{2,1,0:T(8,128)(2,1)S(1)}, bf16[4,512,128]{2,1,0:T(8,128)(2,1)}, u32[]{:S(2)}) copy-start(bf16[4,512,128]{2,1,0:T(8,128)(2,1)} %param.5) | copy-start | bytes 1572868
  302.2 1.0 copy-start.3
  302.2 1.3 copy-start.4
